TPU v7x, 256 devices: a whole 4x4x8 slice. The times are simulated.
256 devices in a mesh: segment: 4 (over x), dp: 64 (over z, y, core).
Axes of the slice: x: 4, y: 4, z: 8, core: 2. Of those that a mesh axis runs over, the one named last changes fastest.
Arguments:
- x_saved: bfloat16 [4, 8192, 1536], P('segment', 'dp'), may hold values from -6 to 6
- gains: float32 [4, 1536], P('segment'), may hold values from 0.1 to 1.9
- w_in: bfloat16 [4, 1536, 3072], P('segment', 'dp'), may hold values from -0.15625 to 0.15625
- w_out: bfloat16 [4, 3072, 1536], P('segment', None, 'dp'), may hold values from -0.109375 to 0.109375
- cotangent: bfloat16 [8192, 1536], P('dp'), may hold values from -6 to 6
- lengths: int32 [64], replicated, may hold values from 1 to 256, 8192 in all
Outputs:
- grads: bfloat16 [4, 8192, 1536], P('segment', 'dp')
- gain_grads: float32 [4, 1536], P('segment')
All inputs are finite; a program needn't handle non-finite values.
Results may differ from a plain program's by a relative error of at most 0.0075.
Values may be sent and summed in bfloat16 or wider, within the bound.
No kernel may reach another device: no remote copies, remote signals or barrier semaphores. Data moves between devices by JAX's collectives and lax.ppermute only.
A program may use at most 128 MiB of HBM per device.

v0:
```python
import jax
import jax.numpy as jnp
from jax import lax
from jax.sharding import PartitionSpec as P


def passed_along(x, axis, by):
    length = lax.axis_size(axis)
    pairs = [(i, i + by) for i in range(length) if 0 <= i + by < length]
    return lax.ppermute(x, axis, pairs)


def on_device(x_saved, gains, w_in, w_out, cotangent, lengths):
    rows = cotangent.shape[0]
    width = cotangent.shape[1]
    ends = jnp.cumsum(lengths)
    position = lax.axis_index("dp") * rows + jnp.arange(rows, dtype=jnp.int32)
    utter_hit = (position[:, None] >= ends[None, :]).astype(jnp.int32)
    utter = jnp.sum(utter_hit, 1)
    onehot = (utter[:, None] == jnp.arange(lengths.shape[0], dtype=jnp.int32)[None, :]).astype(
        jnp.int32
    )
    tok_len = jnp.sum(onehot * lengths[None, :], 1).astype(jnp.float32)
    weight = 2.0 * rows / (tok_len + rows)
    current = (cotangent.astype(jnp.float32) * weight[:, None]).astype(jnp.bfloat16)
    xf = x_saved[0].astype(jnp.float32)
    centered_input = xf - jnp.mean(xf, -1, keepdims=True)
    variance = jnp.mean(centered_input * centered_input, -1, keepdims=True)
    inverse_deviation = lax.rsqrt(variance + 1e-05)
    standardized_input = centered_input * inverse_deviation
    gain_vector = gains[0]
    normalized_input = (standardized_input * gain_vector).astype(jnp.bfloat16)
    w_first, w_second = (
        lax.all_gather(w_in[0], "dp", axis=0, tiled=True),
        lax.all_gather(w_out[0], "dp", axis=1, tiled=True),
    )

    def project_all(normed_rows, grad_in):
        hidden = jnp.dot(normed_rows, w_first, preferred_element_type=jnp.float32)
        up_grad = jnp.dot(grad_in, w_second.T, preferred_element_type=jnp.float32)
        sig = jax.nn.sigmoid(hidden)
        hid_grad = (0.5 * up_grad * (sig + hidden * sig * (1.0 - sig))).astype(jnp.bfloat16)
        return jnp.dot(hid_grad, w_first.T, preferred_element_type=jnp.float32)

    def block_back():

        def run(grad_in):
            norm_gradient = project_all(normalized_input, grad_in)
            gain_partial = jnp.sum(norm_gradient * standardized_input, 0)
            gain_scaled = norm_gradient * gain_vector
            backward_result = inverse_deviation * (
                gain_scaled
                - jnp.mean(gain_scaled, -1, keepdims=True)
                - standardized_input * jnp.mean(gain_scaled * standardized_input, -1, keepdims=True)
            )
            return (
                (grad_in.astype(jnp.float32) + backward_result).astype(jnp.bfloat16),
                gain_partial,
            )

        return run

    def pass_through(grad_in):
        return (grad_in, jnp.zeros((width,), jnp.float32))

    segments = lax.axis_size("segment")
    my_segment = lax.axis_index("segment")
    gain_local = jnp.zeros((width,), jnp.float32)
    result = current
    for level in range(segments - 1, -1, -1):
        mine = my_segment == level
        updated, gain_partial = lax.cond(mine, block_back(), pass_through, current)
        result = jnp.where(mine, updated, result)
        gain_local = jnp.where(mine, gain_partial, gain_local)
        if level > 0:
            current = passed_along(updated, "segment", -1)
    gain_total = lax.psum(gain_local, "dp")
    return (result[None], gain_total[None])


def solution(mesh):
    in_specs = (
        P("segment", "dp", None),
        P("segment", None),
        P("segment", "dp", None),
        P("segment", None, "dp"),
        P("dp", None),
        P(),
    )
    out_specs = (P("segment", "dp", None), P("segment", None))
    return jax.shard_map(
        on_device, mesh=mesh, in_specs=in_specs, out_specs=out_specs, check_vma=False
    )
```

profile of v0, /device:TPU:1, one launch (start us, length us, event | category | flops | bytes accessed | tf_op | source)
XLA Modules:
  0.0 432.3 jit_solution(9842427514506412659)
XLA Ops:
  7.2 0.0 all-gather.7.cloned.1.call-start
  7.2 0.7 all-gather.7.cloned.1.call-update
  7.9 0.0 all-gather.5.cloned.1.call-start
  7.9 0.7 all-gather.5.cloned.1.call-update
  8.7 0.7 copy.17
  9.4 0.1 reduce-window.8
  9.5 0.1 reduce.5
  9.6 0.7 reduce.6
  10.3 0.1 convert_reduce_fusion.1
  10.4 0.7 select_reduce_fusion
  11.2 0.0 copy-start
  11.2 1.1 convert_reduce_fusion
  12.3 1.2 fusion.23
  13.6 0.0 copy-start.4
  13.6 1.5 fusion.21
  15.1 84.0 %all-gather.7.cloned.1.call-done = bf16[1,1536,3072]{2,1,0:T(8,128)(2,1)} async-done(((bf16[1,24,3072]{2,1,0:T(8,128)(2,1)}), bf16[1,1536,3072]{2,1,0:T(8,128)(2,1)}) %all-gather.7.cloned.1.call-update) | async-done | bytes 9437200 | tf_op jit(solution)/shard_map/all_gather | solution.py:34
  99.1 84.1 %all-gather.5.cloned.1.call-done = bf16[1,3072,1536]{1,2,0:T(8,128)(2,1)} async-done(((bf16[1,3072,24]{1,2,0:T(8,128)(2,1)}), bf16[1,3072,1536]{1,2,0:T(8,128)(2,1)}) %all-gather.5.cloned.1.call-update) | async-done | bytes 9437200 | tf_op jit(solution)/shard_map/all_gather | solution.py:35
  183.2 0.0 copy-done
  183.2 0.0 copy-done.4
  183.2 0.6 conditional.4
  183.3 0.6 broadcast.129
  183.9 1.3 collective-permute-start
  185.1 11.0 %collective-permute-done = bf16[128,1536]{1,0:T(8,128)(2,1)S(1)} collective-permute-done((bf16[128,1536]{1,0:T(8,128)(2,1)S(1)}, bf16[128,1536]{1,0:T(8,128)(2,1)S(1)}, u32[]{:S(2)}, u32[]{:S(2)}) %collective-permute-start) | collective-permute-done | bytes 393248 | tf_op jit(solution)/shard_map/ppermute | solution.py:10
  196.2 0.0 copy-start.2
  196.2 1.3 collective-permute-start.1
  197.4 10.1 %collective-permute-done.1 = bf16[128,1536]{1,0:T(8,128)(2,1)S(1)} collective-permute-done((bf16[128,1536]{1,0:T(8,128)(2,1)S(1)}, bf16[128,1536]{1,0:T(8,128)(2,1)S(1)}, u32[]{:S(2)}, u32[]{:S(2)}) %collective-permute-start.1) | collective-permute-done | bytes 393248 | tf_op jit(solution)/shard_map/ppermute | solution.py:10
  207.6 0.0 copy-done.2
  207.6 0.6 conditional.6
  207.6 0.6 broadcast.137
  208.2 1.3 collective-permute-start.2
  209.5 66.8 %collective-permute-done.2 = bf16[128,1536]{1,0:T(8,128)(2,1)S(1)} collective-permute-done((bf16[128,1536]{1,0:T(8,128)(2,1)S(1)}, bf16[128,1536]{1,0:T(8,128)(2,1)S(1)}, u32[]{:S(2)}, u32[]{:S(2)}) %collective-permute-start.2) | collective-permute-done | bytes 393248 | tf_op jit(solution)/shard_map/ppermute | solution.py:10
  276.3 0.0 copy-start.1
  276.3 0.0 copy-start.3
  276.3 20.4 %conditional.7 = (bf16[128,1536]{1,0:T(8,128)(2,1)S(1)}, f32[1536]{0:T(1024)S(1)}) conditional(s32[]{:T(128)} %convert_element_type.77, bf16[128,1536]{1,0:T(8,128)(2,1)S(1)} %collective-permute-done.2, (bf16[128,1536]{1,0:T(8,128)(2,1)S(1)}, f32[128,1]{0,1:T(1,128)}, bf16[3072,1536]{0,1:T(8,128)(2,1)}, bf16[128,1536]{1,0:T(8,128)(2,1)S(1)}, ...), branch_computations={%region_20.21_spmd, %region_21.25_spmd} | conditional | flops 3630562048 | bytes 36213296 | solution.py:72
  276.3 6.2 %fusion.28 = f32[128,3072]{1,0:T(8,128)} fusion(bf16[128,1536]{1,0:T(8,128)(2,1)S(1)} %get-tuple-element.84, bf16[1536,3072]{1,0:T(8,128)(2,1)} %get-tuple-element.85), kind=kOutput, calls=%fused_computation.69 | convolution fusion | flops 1207959552 | bytes 11403264 | tf_op jit(solution)/shard_map/cond/branch_1_fun/dot_general | solution.py:39
  282.5 0.0 copy-start.7
  282.5 12.7 %multiply_reduce_fusion.9 = (f32[1536]{0:T(1024)S(1)}, f32[128]{0:T(128)S(1)}, f32[128]{0:T(128)S(1)}, f32[128,1536]{1,0:T(8,128)}) fusion(f32[128,1536]{1,0:T(8,128)S(1)} %get-tuple-element.87, f32[1536]{0:T(1024)S(1)} %reduce.4, bf16[1536,3072]{1,0:T(8,128)(2,1)} %get-tuple-element.85, bf16[128,1536]{1,0:T(8,128)(2,1)S(1)} %get-tuple-element.81, ...), kind=kOutput, calls=%fused_computation.39 | convolution fusion | flops 2421029376 | bytes 22426624 | tf_op jit(solution)/shard_map/cond/branch_1_fun/dot_general | solution.py:43
  295.2 0.0 copy-done.7
  295.2 1.4 add_convert_fusion.3
  296.7 0.0 copy-done.1
  296.7 0.0 copy-done.3
  296.7 0.8 select_bitcast_fusion
  297.5 128.0 %psum.7 = f32[1,1536]{1,0:T(1,128)} all-reduce(f32[1,1536]{1,0:T(1,128)S(1)} %broadcast_in_dim.5), channel_id=1, replica_groups=mesh['segment'=4,'dp'=64] {'dp'}, use_global_device_ids=true, to_apply=%region_25.26 | all-reduce | flops 1536 | bytes 12288 | tf_op jit(solution)/shard_map/psum | solution.py:77
  (11 shorter events, 0.1 us)
Async XLA Ops:
  7.2 92.0 %all-gather.7.cloned.1.call-start = ((), (), s32[]{:S(2)}) async-start(), calls=%async_computation.1 | async-start | bytes 9584640 | tf_op jit(solution)/shard_map/all_gather | solution.py:34
  7.9 175.3 %all-gather.5.cloned.1.call-start = ((), (), s32[]{:S(2)}) async-start(), calls=%async_computation | async-start | bytes 9584640 | tf_op jit(solution)/shard_map/all_gather | solution.py:35
  11.2 172.0 %copy-start = (f32[1,1536]{1,0:T(1,128)S(1)}, f32[1,1536]{1,0:T(1,128)}, u32[]{:S(2)}) copy-start(f32[1,1536]{1,0:T(1,128)} %param.15) | copy-start | bytes 18436
  13.6 169.6 %copy-start.4 = (f32[128,1]{0,1:T(1,128)}, f32[128,1]{0,1:T(1,128)S(1)}, u32[]{:S(2)}) copy-start(f32[128,1]{0,1:T(1,128)S(1)} %get-tuple-element.189) | copy-start | bytes 1540
  183.9 12.3 %collective-permute-start = (bf16[128,1536]{1,0:T(8,128)(2,1)S(1)}, bf16[128,1536]{1,0:T(8,128)(2,1)S(1)}, u32[]{:S(2)}, u32[]{:S(2)}) collective-permute-start(bf16[128,1536]{1,0:T(8,128)(2,1)S(1)} %get-tuple-element.98), channel_id=1, source_target_pairs={{64,0},{128,64},{192,128},{65,1},{129,65},{193,129},{66,2},{130,66... | collective-permute-start | bytes 1179656 | tf_op jit(solution)/shard_map/ppermute | solution.py:10
  196.2 11.4 %copy-start.2 = (f32[1536]{0:T(1024)}, f32[1536]{0:T(1024)S(1)}, u32[]{:S(2)}) copy-start(f32[1536]{0:T(1024)S(1)} %get-tuple-element.104) | copy-start | bytes 18436
  196.2 11.4 %collective-permute-start.1 = (bf16[128,1536]{1,0:T(8,128)(2,1)S(1)}, bf16[128,1536]{1,0:T(8,128)(2,1)S(1)}, u32[]{:S(2)}, u32[]{:S(2)}) collective-permute-start(bf16[128,1536]{1,0:T(8,128)(2,1)S(1)} %get-tuple-element.99), channel_id=1, source_target_pairs={{64,0},{128,64},{192,128},{65,1},{129,65},{193,129},{66,2},{130,66... | collective-permute-start | bytes 1179656 | tf_op jit(solution)/shard_map/ppermute | solution.py:10
  208.2 68.1 %collective-permute-start.2 = (bf16[128,1536]{1,0:T(8,128)(2,1)S(1)}, bf16[128,1536]{1,0:T(8,128)(2,1)S(1)}, u32[]{:S(2)}, u32[]{:S(2)}) collective-permute-start(bf16[128,1536]{1,0:T(8,128)(2,1)S(1)} %get-tuple-element.100), channel_id=1, source_target_pairs={{64,0},{128,64},{192,128},{65,1},{129,65},{193,129},{66,2},{130,66... | collective-permute-start | bytes 1179656 | tf_op jit(solution)/shard_map/ppermute | solution.py:10
  276.3 20.4 %copy-start.1 = (f32[1536]{0:T(1024)S(1)}, f32[1536]{0:T(1024)}, u32[]{:S(2)}) copy-start(f32[1536]{0:T(1024)} %get-tuple-element.105) | copy-start | bytes 18436
  276.3 20.4 %copy-start.3 = (f32[1536]{0:T(1024)S(1)}, f32[1536]{0:T(1024)}, u32[]{:S(2)}) copy-start(f32[1536]{0:T(1024)} %copy-done.2) | copy-start | bytes 18436
  282.5 12.7 %copy-start.7 = (f32[128,1]{0,1:T(1,128)S(1)}, f32[128,1]{0,1:T(1,128)}, u32[]{:S(2)}) copy-start(f32[128,1]{0,1:T(1,128)} %get-tuple-element.82) | copy-start | bytes 1540 | tf_op jit(solution)/shard_map/cond
Sparse Core Ops, SparseCore 0:
  10.7 88.3 all-gather.6
  101.8 81.3 all-gather.4
where the time goes:
time: 433 us; the launch traced here: 432 us
  waiting for transfers between devices  257 us (59%)
  blocking collectives  128 us (30%)
  matrix products  18.9 us (4%)
  between operations  14.2 us (3%)
  other arithmetic  7.95 us (2%)
    psum x1, blocking collectives, on_device(): gain_total = lax.psum(gain_local, 'dp')  128 us
    ppermute x3, waiting for transfers between devices, passed_along(): return lax.ppermute(x, axis, pairs)  87.9 us
    all_gather x1, waiting for transfers between devices, on_device(): lax.all_gather(w_out[0], 'dp', axis=1, tiled=True)  84.1 us
    all_gather x1, waiting for transfers between devices, on_device(): lax.all_gather(w_in[0], 'dp', axis=0, tiled=True)  84 us
    dot_general x1, matrix products, project_all(): return jnp.dot(hid_grad, w_first.T, preferred_element_type=jnp.float32)  12.7 us
  transfers between devices with their start and end apart: 5, of which 5 were waited for; matrix products, arithmetic and copies ran while one was open for 1% of the time, Pallas kernels for 0%

commit v1 on v0

--- a/solution.py
+++ b/solution.py
@@ -74,7 +74,7 @@
         gain_local = jnp.where(mine, gain_partial, gain_local)
         if level > 0:
             current = passed_along(updated, "segment", -1)
-    gain_total = lax.psum(gain_local, "dp")
+    gain_total = jnp.sum(lax.all_gather(gain_local, "dp"), axis=0)
     return (result[None], gain_total[None])
 
 

time: 433 us -> 355 us (0.82)
  blocking collectives: 128 us -> 49.4 us
    psum x1 -> x0, blocking collectives: 128 us -> none  [on_device(): gain_total = lax.psum(gain_local, 'dp')]
    all_gather x0 -> x1, blocking collectives: none -> 49.4 us  [on_device(): gain_total = jnp.sum(lax.all_gather(gain_local, 'dp'), axis=0)]
  transfers between devices with their start and end apart: 5 -> 5, of which waited for: 5 -> 5; matrix products, arithmetic and copies ran while one was open for 1% -> 2% of each run, Pallas kernels for 0% -> 0%
where the time goes in v1:
time: 355 us
  waiting for transfers between devices  257 us (72%)
  blocking collectives  49.4 us (14%)
  matrix products  18.9 us (5%)
  between operations  14.2 us (4%)
  other arithmetic  8.2 us (2%)
  starting transfers between devices  3.92 us (1%)
    ppermute x3, waiting for transfers between devices, passed_along(): return lax.ppermute(x, axis, pairs)  87.9 us
    all_gather x1, waiting for transfers between devices, on_device(): lax.all_gather(w_out[0], 'dp', axis=1, tiled=True)  84.1 us
    all_gather x1, waiting for transfers between devices, on_device(): lax.all_gather(w_in[0], 'dp', axis=0, tiled=True)  84 us
    all_gather x1, blocking collectives, on_device(): gain_total = jnp.sum(lax.all_gather(gain_local, 'dp'), axis=0)  49.4 us
    dot_general x1, matrix products, project_all(): return jnp.dot(hid_grad, w_first.T, preferred_element_type=jnp.float32)  12.7 us
  transfers between devices with their start and end apart: 5, of which 5 were waited for; matrix products, arithmetic and copies ran while one was open for 2% of the time, Pallas kernels for 0%

profile of v1, /device:TPU:1, one launch (start us, length us, event | category | flops | bytes accessed | tf_op | source)
XLA Modules:
  0.0 354.6 jit_solution(9302220753078983392)
XLA Ops:
  7.2 0.0 all-gather.9.cloned.1.call-start
  7.2 0.7 all-gather.9.cloned.1.call-update
  7.9 0.0 all-gather.7.cloned.1.call-start
  7.9 0.7 all-gather.7.cloned.1.call-update
  8.7 0.7 copy.17
  9.4 0.1 reduce-window.8
  9.5 0.1 reduce.6
  9.6 0.7 reduce.7
  10.3 0.1 convert_reduce_fusion.1
  10.4 0.7 select_reduce_fusion
  11.2 0.0 copy-start
  11.2 1.1 convert_reduce_fusion
  12.3 1.2 fusion.23
  13.6 0.0 copy-start.4
  13.6 1.5 fusion.21
  15.1 84.0 %all-gather.9.cloned.1.call-done = bf16[1,1536,3072]{2,1,0:T(8,128)(2,1)} async-done(((bf16[1,24,3072]{2,1,0:T(8,128)(2,1)}), bf16[1,1536,3072]{2,1,0:T(8,128)(2,1)}) %all-gather.9.cloned.1.call-update) | async-done | bytes 9437200 | tf_op jit(solution)/shard_map/all_gather | solution.py:34
  99.1 84.1 %all-gather.7.cloned.1.call-done = bf16[1,3072,1536]{1,2,0:T(8,128)(2,1)} async-done(((bf16[1,3072,24]{1,2,0:T(8,128)(2,1)}), bf16[1,3072,1536]{1,2,0:T(8,128)(2,1)}) %all-gather.7.cloned.1.call-update) | async-done | bytes 9437200 | tf_op jit(solution)/shard_map/all_gather | solution.py:35
  183.2 0.0 copy-done
  183.2 0.0 copy-done.4
  183.2 0.6 conditional.4
  183.3 0.6 broadcast.129
  183.9 1.3 collective-permute-start
  185.1 11.0 %collective-permute-done = bf16[128,1536]{1,0:T(8,128)(2,1)S(1)} collective-permute-done((bf16[128,1536]{1,0:T(8,128)(2,1)S(1)}, bf16[128,1536]{1,0:T(8,128)(2,1)S(1)}, u32[]{:S(2)}, u32[]{:S(2)}) %collective-permute-start) | collective-permute-done | bytes 393248 | tf_op jit(solution)/shard_map/ppermute | solution.py:10
  196.2 0.0 copy-start.2
  196.2 1.3 collective-permute-start.1
  197.4 10.1 %collective-permute-done.1 = bf16[128,1536]{1,0:T(8,128)(2,1)S(1)} collective-permute-done((bf16[128,1536]{1,0:T(8,128)(2,1)S(1)}, bf16[128,1536]{1,0:T(8,128)(2,1)S(1)}, u32[]{:S(2)}, u32[]{:S(2)}) %collective-permute-start.1) | collective-permute-done | bytes 393248 | tf_op jit(solution)/shard_map/ppermute | solution.py:10
  207.6 0.0 copy-done.2
  207.6 0.6 conditional.6
  207.6 0.6 broadcast.137
  208.2 1.3 collective-permute-start.2
  209.5 66.8 %collective-permute-done.2 = bf16[128,1536]{1,0:T(8,128)(2,1)S(1)} collective-permute-done((bf16[128,1536]{1,0:T(8,128)(2,1)S(1)}, bf16[128,1536]{1,0:T(8,128)(2,1)S(1)}, u32[]{:S(2)}, u32[]{:S(2)}) %collective-permute-start.2) | collective-permute-done | bytes 393248 | tf_op jit(solution)/shard_map/ppermute | solution.py:10
  276.3 0.0 copy-start.1
  276.3 0.0 copy-start.3
  276.3 20.4 %conditional.7 = (bf16[128,1536]{1,0:T(8,128)(2,1)S(1)}, f32[1536]{0:T(1024)S(1)}) conditional(s32[]{:T(128)} %convert_element_type.77, bf16[128,1536]{1,0:T(8,128)(2,1)S(1)} %collective-permute-done.2, (bf16[128,1536]{1,0:T(8,128)(2,1)S(1)}, f32[128,1]{0,1:T(1,128)}, bf16[3072,1536]{0,1:T(8,128)(2,1)}, bf16[128,1536]{1,0:T(8,128)(2,1)S(1)}, ...), branch_computations={%region_20.21_spmd, %region_21.25_spmd} | conditional | flops 3630562048 | bytes 36213296 | solution.py:72
  276.3 6.2 %fusion.28 = f32[128,3072]{1,0:T(8,128)} fusion(bf16[128,1536]{1,0:T(8,128)(2,1)S(1)} %get-tuple-element.84, bf16[1536,3072]{1,0:T(8,128)(2,1)} %get-tuple-element.85), kind=kOutput, calls=%fused_computation.69 | convolution fusion | flops 1207959552 | bytes 11403264 | tf_op jit(solution)/shard_map/cond/branch_1_fun/dot_general | solution.py:39
  282.5 0.0 copy-start.7
  282.5 12.7 %multiply_reduce_fusion.9 = (f32[1536]{0:T(1024)S(1)}, f32[128]{0:T(128)S(1)}, f32[128]{0:T(128)S(1)}, f32[128,1536]{1,0:T(8,128)}) fusion(f32[128,1536]{1,0:T(8,128)S(1)} %get-tuple-element.87, f32[1536]{0:T(1024)S(1)} %reduce.5, bf16[1536,3072]{1,0:T(8,128)(2,1)} %get-tuple-element.85, bf16[128,1536]{1,0:T(8,128)(2,1)S(1)} %get-tuple-element.81, ...), kind=kOutput, calls=%fused_computation.39 | convolution fusion | flops 2421029376 | bytes 22426624 | tf_op jit(solution)/shard_map/cond/branch_1_fun/dot_general | solution.py:43
  295.2 0.0 copy-done.7
  295.2 1.4 add_convert_fusion.3
  296.7 0.0 copy-done.1
  296.7 0.0 copy-done.3
  296.7 0.8 select_bitcast_fusion
  297.5 49.4 %all-gather.3 = f32[64,1,1536]{2,1,0:T(1,128)S(1)} all-gather(f32[1,1,1536]{2,1,0:T(1,128)S(1)} %reshape.102), channel_id=4, replica_groups=mesh['segment'=4,'dp'=64] {'dp'}, dimensions={0}, use_global_device_ids=true | all-gather | bytes 399360 | tf_op jit(solution)/shard_map/all_gather | solution.py:77
  346.9 0.2 reduce_sum.157
  347.2 0.6 broadcast_in_dim.5
  (11 shorter events, 0.1 us)
Async XLA Ops:
  7.2 92.0 %all-gather.9.cloned.1.call-start = ((), (), s32[]{:S(2)}) async-start(), calls=%async_computation.1 | async-start | bytes 9584640 | tf_op jit(solution)/shard_map/all_gather | solution.py:34
  7.9 175.3 %all-gather.7.cloned.1.call-start = ((), (), s32[]{:S(2)}) async-start(), calls=%async_computation | async-start | bytes 9584640 | tf_op jit(solution)/shard_map/all_gather | solution.py:35
  11.2 172.0 %copy-start = (f32[1,1536]{1,0:T(1,128)S(1)}, f32[1,1536]{1,0:T(1,128)}, u32[]{:S(2)}) copy-start(f32[1,1536]{1,0:T(1,128)} %param.15) | copy-start | bytes 18436
  13.6 169.6 %copy-start.4 = (f32[128,1]{0,1:T(1,128)}, f32[128,1]{0,1:T(1,128)S(1)}, u32[]{:S(2)}) copy-start(f32[128,1]{0,1:T(1,128)S(1)} %get-tuple-element.189) | copy-start | bytes 1540
  183.9 12.3 %collective-permute-start = (bf16[128,1536]{1,0:T(8,128)(2,1)S(1)}, bf16[128,1536]{1,0:T(8,128)(2,1)S(1)}, u32[]{:S(2)}, u32[]{:S(2)}) collective-permute-start(bf16[128,1536]{1,0:T(8,128)(2,1)S(1)} %get-tuple-element.98), channel_id=1, source_target_pairs={{64,0},{128,64},{192,128},{65,1},{129,65},{193,129},{66,2},{130,66... | collective-permute-start | bytes 1179656 | tf_op jit(solution)/shard_map/ppermute | solution.py:10
  196.2 11.4 %copy-start.2 = (f32[1536]{0:T(1024)}, f32[1536]{0:T(1024)S(1)}, u32[]{:S(2)}) copy-start(f32[1536]{0:T(1024)S(1)} %get-tuple-element.104) | copy-start | bytes 18436
  196.2 11.4 %collective-permute-start.1 = (bf16[128,1536]{1,0:T(8,128)(2,1)S(1)}, bf16[128,1536]{1,0:T(8,128)(2,1)S(1)}, u32[]{:S(2)}, u32[]{:S(2)}) collective-permute-start(bf16[128,1536]{1,0:T(8,128)(2,1)S(1)} %get-tuple-element.99), channel_id=1, source_target_pairs={{64,0},{128,64},{192,128},{65,1},{129,65},{193,129},{66,2},{130,66... | collective-permute-start | bytes 1179656 | tf_op jit(solution)/shard_map/ppermute | solution.py:10
  208.2 68.1 %collective-permute-start.2 = (bf16[128,1536]{1,0:T(8,128)(2,1)S(1)}, bf16[128,1536]{1,0:T(8,128)(2,1)S(1)}, u32[]{:S(2)}, u32[]{:S(2)}) collective-permute-start(bf16[128,1536]{1,0:T(8,128)(2,1)S(1)} %get-tuple-element.100), channel_id=1, source_target_pairs={{64,0},{128,64},{192,128},{65,1},{129,65},{193,129},{66,2},{130,66... | collective-permute-start | bytes 1179656 | tf_op jit(solution)/shard_map/ppermute | solution.py:10
  276.3 20.4 %copy-start.1 = (f32[1536]{0:T(1024)S(1)}, f32[1536]{0:T(1024)}, u32[]{:S(2)}) copy-start(f32[1536]{0:T(1024)} %get-tuple-element.105) | copy-start | bytes 18436
  276.3 20.4 %copy-start.3 = (f32[1536]{0:T(1024)S(1)}, f32[1536]{0:T(1024)}, u32[]{:S(2)}) copy-start(f32[1536]{0:T(1024)} %copy-done.2) | copy-start | bytes 18436
  282.5 12.7 %copy-start.7 = (f32[128,1]{0,1:T(1,128)S(1)}, f32[128,1]{0,1:T(1,128)}, u32[]{:S(2)}) copy-start(f32[128,1]{0,1:T(1,128)} %get-tuple-element.82) | copy-start | bytes 1540 | tf_op jit(solution)/shard_map/cond
Sparse Core Ops, SparseCore 0:
  10.7 88.3 all-gather.8
  101.8 81.3 all-gather.6
